TPU v7x, 32 devices: a whole 2x2x4 slice. The times are simulated.
32 devices in a mesh: aux: 4 (over y, x), pair: 8 (over z, core).
Axes of the slice: x: 2, y: 2, z: 4, core: 2. Of those that a mesh axis runs over, the one named last changes fastest.
Arguments:
- three_index: bfloat16 [32, 2048, 256], P('pair', 'aux'), may hold values from -6 to 6
- pno_coef: bfloat16 [128, 2, 256, 192], P('pair'), may hold values from -0.375 to 0.375
- pair_orbitals: int32 [128, 2], P('pair'), may hold values from 0 to 31, as said below
- natural_orbital_class: int32 [128], P('pair'), may hold values from 0 to 3
- pno_energy: float32 [128, 192], P('pair'), may hold values from 0.5 to 4
- margin: bfloat16 [128, 2, 192, 192], P('pair'), may hold values from -0.4375 to 0.4375
- neighbour_pairs: int32 [128, 2], P('pair'), may hold values from 0 to 127, as said below
- fock_coupling: float32 [128, 2], P('pair'), may hold values from -0.9 to 0.9
Outputs:
- amplitudes: float32 [128, 192, 192], P('pair')
- residual: float32 [128, 192, 192], P('pair')
Inputs may be any that keep to these rules, and one draw needn't show every extreme that they name: `pair_orbitals`: column 0 names an orbital of the pair's own block of 4 orbitals (pair p's block is p // 16); column 1 names one of that block or of the block just before or after it. `neighbour_pairs`: each entry names another pair of the pair's own block of 16 pairs or of the block just before or after it.
All inputs are finite; a program needn't handle non-finite values.
Results may differ from a plain program's by a relative error of at most 0.0032.
Values may be sent and summed in bfloat16 or wider, within the bound.
No kernel may reach another device: no remote copies, remote signals or barrier semaphores. Data moves between devices by JAX's collectives and lax.ppermute only.
A program may use at most 128 MiB of HBM per device.

v0:
```python
import jax
import jax.numpy as jnp
from jax import lax
from jax.sharding import PartitionSpec as P

NPNO = 192
ITERS = 2


def with_halo(cells, sides, width):
    for axis, dim in sides:
        count = lax.axis_size(axis)
        ends = count - 1
        head = lax.slice_in_dim(cells, 0, width, axis=dim)
        tail = lax.slice_in_dim(cells, cells.shape[dim] - width, cells.shape[dim], axis=dim)
        cells = jnp.concatenate(
            [
                lax.ppermute(tail, axis, [(i, (i + 1) % count) for i in range(ends)]),
                cells,
                lax.ppermute(head, axis, [((i + 1) % count, i) for i in range(ends)]),
            ],
            axis=dim,
        )
    return cells


def class_mask(natural_orbital_class):
    counts = jnp.where(
        natural_orbital_class == 0,
        NPNO // 6,
        jnp.where(
            natural_orbital_class == 1,
            NPNO // 3,
            jnp.where(natural_orbital_class == 2, 2 * NPNO // 3, NPNO),
        ),
    )
    return jnp.arange(NPNO, dtype=jnp.int32)[None, :] < counts[:, None]


def transformed_product(side_blocks, gathered, weights):
    inner_part = jnp.einsum(
        "pnab,pnbc->pnac", side_blocks, gathered, precision=lax.Precision.HIGHEST
    )
    outer_part = jnp.einsum(
        "pnac,pndc->pnad", inner_part, side_blocks, precision=lax.Precision.HIGHEST
    )
    return jnp.einsum("pn,pnad->pad", weights, outer_part, precision=lax.Precision.HIGHEST)


def iterate(exchange_ints, denominator, coupling):
    amplitudes = jnp.zeros_like(exchange_ints)
    for iteration in range(ITERS):
        current_residual = exchange_ints + denominator * amplitudes
        if iteration > 0:
            current_residual = current_residual - coupling(amplitudes)
        amplitudes = amplitudes - current_residual / denominator
    residual = exchange_ints + denominator * amplitudes - coupling(amplitudes)
    return (amplitudes, residual)


def per_device(
    three_index,
    pno_coef,
    pair_orbitals,
    natural_orbital_class,
    pno_energy,
    margin,
    neighbour_pairs,
    fock_coupling,
):
    occ_dev = three_index.shape[0]
    pair_dev = pno_coef.shape[0]
    position = lax.axis_index("pair")
    natural_orbital_mask = class_mask(natural_orbital_class)
    padded = with_halo(three_index, (("pair", 0),), occ_dev)
    local_orbitals = pair_orbitals - (position - 1) * occ_dev
    leading_block = jnp.take(padded, local_orbitals[:, 0], axis=0)
    trailing_block = jnp.take(padded, local_orbitals[:, 1], axis=0)
    masked_coefficient_rows = jnp.where(
        natural_orbital_mask[:, None, None, :], pno_coef, jnp.zeros((), jnp.bfloat16)
    )
    left_half = jnp.einsum(
        "cyg,cgh->cyh",
        leading_block,
        masked_coefficient_rows[:, 0],
        preferred_element_type=jnp.float32,
    ).astype(jnp.bfloat16)
    right_half = jnp.einsum(
        "cyg,cgh->cyh",
        trailing_block,
        masked_coefficient_rows[:, 1],
        preferred_element_type=jnp.float32,
    ).astype(jnp.bfloat16)
    partial_ints = jnp.einsum(
        "pqa,pqb->pab", left_half, right_half, preferred_element_type=jnp.float32
    )
    mask_float = natural_orbital_mask.astype(jnp.float32)
    exchange_ints = lax.psum(partial_ints, "aux")
    denominator = pno_energy[:, :, None] + pno_energy[:, None, :]
    side_blocks = margin.astype(jnp.float32) * mask_float[:, None, :, None]
    local_rows = neighbour_pairs - (position - 1) * pair_dev

    def coupling(current):
        padded_amps = with_halo(current, (("pair", 0),), pair_dev)
        gathered = jnp.take(padded_amps, local_rows, axis=0)
        return transformed_product(side_blocks, gathered, fock_coupling)

    amplitudes, residual = iterate(exchange_ints, denominator, coupling)
    return (amplitudes, residual)


def solution(mesh):
    return jax.shard_map(
        per_device,
        mesh=mesh,
        in_specs=(
            P("pair", "aux", None),
            P("pair", None, None, None),
            P("pair", None),
            P("pair"),
            P("pair", None),
            P("pair", None, None, None),
            P("pair", None),
            P("pair", None),
        ),
        out_specs=(P("pair", None, None), P("pair", None, None)),
        check_vma=False,
    )
```

profile of v0, /device:TPU:1, one launch (start us, length us, event | category | flops | bytes accessed | tf_op | source)
XLA Modules:
  0.0 342.3 jit_solution(12701743786358412983)
XLA Ops:
  7.2 4.6 %collective-permute-start = (bf16[4,512,256]{2,1,0:T(8,128)(2,1)}, bf16[4,512,256]{2,1,0:T(8,128)(2,1)}, u32[]{:S(2)}, u32[]{:S(2)}) collective-permute-start(bf16[4,512,256]{2,1,0:T(8,128)(2,1)} %param.12), channel_id=1, source_target_pairs={{0,1},{1,2},{2,3},{3,4},{4,5},{5,6},{6,7},{8,9},{9,10},{10,11},{11... | collective-permute-start | bytes 3145736 | tf_op jit(solution)/shard_map/ppermute | solution.py:18
  11.8 1.9 collective-permute-start.1
  15.2 3.4 %broadcast_select_fusion = bf16[16,2,256,192]{2,3,1,0:T(8,128)(2,1)} fusion(bf16[16,2,256,192]{2,3,1,0:T(8,128)(2,1)} %param.13, pred[16,192]{1,0:T(8,128)(4,1)S(1)} %get-tuple-element.13), kind=kLoop, calls=%fused_computation.46 | loop fusion | flops 1572864 | bytes 6294528 | tf_op jit(solution)/shard_map/jit(_where)/select_n | solution.py:79
  18.6 5.2 %collective-permute-done = bf16[4,512,256]{2,1,0:T(8,128)(2,1)} collective-permute-done((bf16[4,512,256]{2,1,0:T(8,128)(2,1)}, bf16[4,512,256]{2,1,0:T(8,128)(2,1)}, u32[]{:S(2)}, u32[]{:S(2)}) %collective-permute-start) | collective-permute-done | bytes 1048608 | tf_op jit(solution)/shard_map/ppermute | solution.py:18
  23.9 1.3 constant_dynamic-update-slice_fusion.2
  25.2 3.0 collective-permute-done.1
  28.3 1.3 constant_dynamic-update-slice_fusion
  29.6 2.8 gather_fusion.1
  32.3 2.8 gather_fusion
  35.1 6.1 %fusion.10 = bf16[16,512,192]{1,2,0:T(8,128)(2,1)} fusion(bf16[16,512,256]{2,1,0:T(8,128)(2,1)} %gather_fusion.1, pred[16]{0:T(512)(128)(4,1)S(1)} %get-tuple-element.10, bf16[16,2,256,192]{2,3,1,0:T(8,128)(2,1)} %broadcast_select_fusion), kind=kOutput, calls=%fused_computation.22 | convolution fusion | flops 807403520 | bytes 8912912 | tf_op jit(solution)/shard_map/cyg,cgh->cyh/dot_general | solution.py:88
  41.2 7.3 %fusion.29 = f32[16,192,192]{2,1,0:T(8,128)} fusion(bf16[16,512,192]{1,2,0:T(8,128)(2,1)} %fusion.10, bf16[16,512,256]{2,1,0:T(8,128)(2,1)} %gather_fusion, pred[16]{0:T(512)(128)(4,1)S(1)} %get-tuple-element.6, bf16[16,2,256,192]{2,3,1,0:T(8,128)(2,1)S(1)} %copy-done.6), kind=kOutput, calls=%fused_computation.41 | convolution fusion | flops 1412956160 | bytes 11272704 | tf_op jit(solution)/shard_map/pqa,pqb->pab/dot_general | solution.py:94
  48.5 87.1 %all-reduce.2.cloned.1.call-done = f32[16,192,192]{2,1,0:T(8,128)} async-done(((f32[16,192,192]{2,1,0:T(8,128)}), f32[16,192,192]{2,1,0:T(8,128)}) %all-reduce.2.cloned.1.call-update) | async-done | bytes 2359312 | tf_op jit(solution)/shard_map/psum | solution.py:98
  135.6 2.3 fusion.17
  137.9 2.6 collective-permute-start.3
  140.5 3.5 %collective-permute-start.2 = (f32[16,192,192]{2,1,0:T(8,128)S(1)}, f32[16,192,192]{2,1,0:T(8,128)}, u32[]{:S(2)}, u32[]{:S(2)}) collective-permute-start(f32[16,192,192]{2,1,0:T(8,128)S(1)} %fusion.17), channel_id=1, source_target_pairs={{0,1},{1,2},{2,3},{3,4},{4,5},{5,6},{6,7},{8,9},{9,10},{10,11},{11... | collective-permute-start | bytes 7077896 | tf_op jit(solution)/shard_map/ppermute | solution.py:18
  144.4 32.2 %collective-permute-done.3 = f32[16,192,192]{2,1,0:T(8,128)} collective-permute-done((f32[16,192,192]{2,1,0:T(8,128)S(1)}, f32[16,192,192]{2,1,0:T(8,128)}, u32[]{:S(2)}, u32[]{:S(2)}) %collective-permute-start.3) | collective-permute-done | bytes 2359328 | tf_op jit(solution)/shard_map/ppermute | solution.py:20
  177.7 7.4 %pad_maximum_fusion = f32[48,192,192]{2,1,0:T(8,128)} fusion(f32[16,192,192]{2,1,0:T(8,128)} %collective-permute-done.3, f32[16,192,192]{2,1,0:T(8,128)S(1)} %fusion.17, f32[16,192,192]{2,1,0:T(8,128)} %collective-permute-done.2), kind=kLoop, calls=%fused_computation.4 | loop fusion | flops 3538944 | bytes 14155776 | tf_op jit(solution)/shard_map/concatenate | solution.py:16
  185.2 7.5 %gather_fusion.2 = f32[32,192,192]{2,1,0:T(8,128)} fusion(f32[48,192,192]{2,1,0:T(8,128)} %pad_maximum_fusion, s32[1024]{0:T(1024)S(1)} %pad_clamp_fusion), kind=kCustom, calls=%fused_computation.1.clone | custom fusion | bytes 9437312 | tf_op jit(solution)/shard_map/jit(_take)/gather | solution.py:105
  192.6 9.5 %fusion.2 = f32[16,2,192,192]{3,2,1,0:T(8,128)S(1)} fusion(f32[16,2,192,192]{3,2,1,0:T(8,128)} %bitcast.26, bf16[16,2,192,192]{3,2,1,0:T(8,128)(2,1)S(1)} %copy-done, f32[16,192]{1,0:T(8,128)S(1)} %get-tuple-element.12, pred[16,2]{1,0:T(8,128)(4,1)S(1)} %copy.14), kind=kOutput, calls=%fused_computation.13 | convolution fusion | flops 2721447936 | bytes 11808800 | tf_op jit(solution)/shard_map/pnab,pnbc->pnac/dot_general | solution.py:41
  202.2 8.0 %fusion.5 = f32[16,2,192,192]{3,2,1,0:T(8,128)S(1)} fusion(f32[16,2,192,192]{3,2,1,0:T(8,128)S(1)} %fusion.2, bf16[16,2,192,192]{3,2,1,0:T(8,128)(2,1)S(1)} %copy-done, f32[16,192]{1,0:T(8,128)S(1)} %get-tuple-element.12), kind=kOutput, calls=%fused_computation.17 | convolution fusion | flops 2720268288 | bytes 11808768 | tf_op jit(solution)/shard_map/pnac,pndc->pnad/dot_general | solution.py:44
  210.2 23.3 %fusion.8 = f32[16,1,192,192]{3,1,2,0:T(1,128)S(1)} fusion(f32[16,2,1,1]{1,2,3,0:T(1,128)S(1)} %copy.19, f32[16,2,192,192]{3,2,1,0:T(8,128)S(1)} %fusion.5), kind=kOutput, calls=%fused_computation.20 | convolution fusion | flops 14155776 | bytes 7078016 | tf_op jit(solution)/shard_map/pn,pnad->pad/dot_general | solution.py:47
  233.6 1.4 fusion.20
  235.0 1.9 collective-permute-start.5
  236.9 4.5 %collective-permute-start.4 = (f32[16,192,192]{2,1,0:T(8,128)S(1)}, f32[16,192,192]{2,1,0:T(8,128)}, u32[]{:S(2)}, u32[]{:S(2)}) collective-permute-start(f32[16,192,192]{2,1,0:T(8,128)S(1)} %fusion.20), channel_id=1, source_target_pairs={{0,1},{1,2},{2,3},{3,4},{4,5},{5,6},{6,7},{8,9},{9,10},{10,11},{11... | collective-permute-start | bytes 7077896 | tf_op jit(solution)/shard_map/ppermute | solution.py:18
  241.4 33.0 %collective-permute-done.5 = f32[16,192,192]{2,1,0:T(8,128)S(1)} collective-permute-done((f32[16,192,192]{2,1,0:T(8,128)S(1)}, f32[16,192,192]{2,1,0:T(8,128)S(1)}, u32[]{:S(2)}, u32[]{:S(2)}) %collective-permute-start.5) | collective-permute-done | bytes 2359328 | tf_op jit(solution)/shard_map/ppermute | solution.py:20
  274.4 1.7 copy-done.5
  276.1 8.5 %pad_maximum_fusion.1 = f32[48,192,192]{2,1,0:T(8,128)} fusion(f32[16,192,192]{2,1,0:T(8,128)} %copy-done.5, f32[16,192,192]{2,1,0:T(8,128)} %copy-done.1, f32[16,192,192]{2,1,0:T(8,128)} %collective-permute-done.4), kind=kLoop, calls=%fused_computation.5 | loop fusion | flops 3538944 | bytes 14155776 | tf_op jit(solution)/shard_map/concatenate | solution.py:16
  284.6 7.3 %gather_fusion.3 = f32[32,192,192]{2,1,0:T(8,128)} fusion(f32[48,192,192]{2,1,0:T(8,128)} %pad_maximum_fusion.1, s32[1024]{0:T(1024)S(1)} %pad_clamp_fusion), kind=kCustom, calls=%fused_computation.3.clone | custom fusion | bytes 9437312 | tf_op jit(solution)/shard_map/jit(_take)/gather | solution.py:105
  291.9 9.7 %fusion = f32[16,2,192,192]{3,2,1,0:T(8,128)S(1)} fusion(f32[16,2,192,192]{3,2,1,0:T(8,128)} %bitcast.25, bf16[16,2,192,192]{3,2,1,0:T(8,128)(2,1)S(1)} %copy-done, f32[16,192]{1,0:T(8,128)S(1)} %get-tuple-element.12, pred[16,2]{1,0:T(8,128)(4,1)S(1)} %copy.14), kind=kOutput, calls=%fused_computation.11 | convolution fusion | flops 2721447936 | bytes 11808800 | tf_op jit(solution)/shard_map/pnab,pnbc->pnac/dot_general | solution.py:41
  301.7 8.0 %fusion.4 = f32[16,2,192,192]{3,2,1,0:T(8,128)S(1)} fusion(f32[16,2,192,192]{3,2,1,0:T(8,128)S(1)} %fusion, bf16[16,2,192,192]{3,2,1,0:T(8,128)(2,1)S(1)} %copy-done, f32[16,192]{1,0:T(8,128)S(1)} %get-tuple-element.12), kind=kOutput, calls=%fused_computation.16 | convolution fusion | flops 2720268288 | bytes 11808768 | tf_op jit(solution)/shard_map/pnac,pndc->pnad/dot_general | solution.py:44
  309.7 23.4 %fusion.6 = f32[16,1,192,192]{3,1,2,0:T(1,128)S(1)} fusion(f32[16,2,1,1]{1,2,3,0:T(1,128)S(1)} %copy.19, f32[16,2,192,192]{3,2,1,0:T(8,128)S(1)} %fusion.4), kind=kOutput, calls=%fused_computation.18 | convolution fusion | flops 14155776 | bytes 7078016 | tf_op jit(solution)/shard_map/pn,pnad->pad/dot_general | solution.py:47
  333.2 2.0 fusion.22
  (37 shorter events, 3.1 us)
Async XLA Ops:
  7.2 128.4 %all-reduce.2.cloned.1.call-start = ((), (), s32[]{:S(2)}) async-start(), calls=%async_computation | async-start | bytes 6291456 | tf_op jit(solution)/shard_map/psum | solution.py:98
  7.2 16.6 %collective-permute-start = (bf16[4,512,256]{2,1,0:T(8,128)(2,1)}, bf16[4,512,256]{2,1,0:T(8,128)(2,1)}, u32[]{:S(2)}, u32[]{:S(2)}) collective-permute-start(bf16[4,512,256]{2,1,0:T(8,128)(2,1)} %param.12), channel_id=1, source_target_pairs={{0,1},{1,2},{2,3},{3,4},{4,5},{5,6},{6,7},{8,9},{9,10},{10,11},{11... | collective-permute-start | bytes 3145736 | tf_op jit(solution)/shard_map/ppermute | solution.py:18
  11.8 16.4 %collective-permute-start.1 = (bf16[4,512,256]{2,1,0:T(8,128)(2,1)}, bf16[4,512,256]{2,1,0:T(8,128)(2,1)}, u32[]{:S(2)}, u32[]{:S(2)}) collective-permute-start(bf16[4,512,256]{2,1,0:T(8,128)(2,1)} %param.12), channel_id=1, source_target_pairs={{1,0},{2,1},{3,2},{4,3},{5,4},{6,5},{7,6},{9,8},{10,9},{11,10},{12... | collective-permute-start | bytes 3145736 | tf_op jit(solution)/shard_map/ppermute | solution.py:20
  15.2 10.0 %copy-start.7 = (bf16[4,512,256]{2,1,0:T(8,128)(2,1)S(1)}, bf16[4,512,256]{2,1,0:T(8,128)(2,1)}, u32[]{:S(2)}) copy-start(bf16[4,512,256]{2,1,0:T(8,128)(2,1)} %param.12) | copy-start | bytes 3145732
  35.1 6.1 %copy-start.6 = (bf16[16,2,256,192]{2,3,1,0:T(8,128)(2,1)S(1)}, bf16[16,2,256,192]{2,3,1,0:T(8,128)(2,1)}, u32[]{:S(2)}) copy-start(bf16[16,2,256,192]{2,3,1,0:T(8,128)(2,1)} %broadcast_select_fusion) | copy-start | bytes 9437188
  48.5 87.1 %copy-start.8 = (f32[16,192]{1,0:T(8,128)S(1)}, f32[16,192]{1,0:T(8,128)}, u32[]{:S(2)}) copy-start(f32[16,192]{1,0:T(8,128)} %param.16) | copy-start | bytes 36868
  48.5 95.5 %copy-start.9 = (s32[16,2]{0,1:T(2,128)S(1)}, s32[16,2]{0,1:T(2,128)}, u32[]{:S(2)}) copy-start(s32[16,2]{0,1:T(2,128)} %param.18) | copy-start | bytes 388
  48.5 95.7 %copy-start.10 = (f32[16,2]{0,1:T(2,128)S(1)}, f32[16,2]{0,1:T(2,128)}, u32[]{:S(2)}) copy-start(f32[16,2]{0,1:T(2,128)} %param.19) | copy-start | bytes 388
  137.9 38.7 %collective-permute-start.3 = (f32[16,192,192]{2,1,0:T(8,128)S(1)}, f32[16,192,192]{2,1,0:T(8,128)}, u32[]{:S(2)}, u32[]{:S(2)}) collective-permute-start(f32[16,192,192]{2,1,0:T(8,128)S(1)} %fusion.17), channel_id=1, source_target_pairs={{1,0},{2,1},{3,2},{4,3},{5,4},{6,5},{7,6},{9,8},{10,9},{11,10},{12... | collective-permute-start | bytes 7077896 | tf_op jit(solution)/shard_map/ppermute | solution.py:20
  140.5 37.2 %collective-permute-start.2 = (f32[16,192,192]{2,1,0:T(8,128)S(1)}, f32[16,192,192]{2,1,0:T(8,128)}, u32[]{:S(2)}, u32[]{:S(2)}) collective-permute-start(f32[16,192,192]{2,1,0:T(8,128)S(1)} %fusion.17), channel_id=1, source_target_pairs={{0,1},{1,2},{2,3},{3,4},{4,5},{5,6},{6,7},{8,9},{9,10},{10,11},{11... | collective-permute-start | bytes 7077896 | tf_op jit(solution)/shard_map/ppermute | solution.py:18
  185.2 7.5 %copy-start = (bf16[16,2,192,192]{3,2,1,0:T(8,128)(2,1)S(1)}, bf16[16,2,192,192]{3,2,1,0:T(8,128)(2,1)}, u32[]{:S(2)}) copy-start(bf16[16,2,192,192]{3,2,1,0:T(8,128)(2,1)} %param.17) | copy-start | bytes 7077892
  210.2 23.4 %copy-start.3 = (f32[16,192,192]{2,1,0:T(8,128)S(1)}, f32[16,192,192]{2,1,0:T(8,128)}, u32[]{:S(2)}) copy-start(f32[16,192,192]{2,1,0:T(8,128)} %all-reduce.2.cloned.1.call-done) | copy-start | bytes 7077892
  235.0 1.9 copy-start.1
  235.0 39.4 %collective-permute-start.5 = (f32[16,192,192]{2,1,0:T(8,128)S(1)}, f32[16,192,192]{2,1,0:T(8,128)S(1)}, u32[]{:S(2)}, u32[]{:S(2)}) collective-permute-start(f32[16,192,192]{2,1,0:T(8,128)S(1)} %fusion.20), channel_id=1, source_target_pairs={{1,0},{2,1},{3,2},{4,3},{5,4},{6,5},{7,6},{9,8},{10,9},{11,10},{12... | collective-permute-start | bytes 7077896 | tf_op jit(solution)/shard_map/ppermute | solution.py:20
  236.9 39.2 %collective-permute-start.4 = (f32[16,192,192]{2,1,0:T(8,128)S(1)}, f32[16,192,192]{2,1,0:T(8,128)}, u32[]{:S(2)}, u32[]{:S(2)}) collective-permute-start(f32[16,192,192]{2,1,0:T(8,128)S(1)} %fusion.20), channel_id=1, source_target_pairs={{0,1},{1,2},{2,3},{3,4},{4,5},{5,6},{6,7},{8,9},{9,10},{10,11},{11... | collective-permute-start | bytes 7077896 | tf_op jit(solution)/shard_map/ppermute | solution.py:18
  274.4 1.7 copy-start.5
  309.7 23.5 %copy-start.2 = (f32[16,192,192]{2,1,0:T(8,128)S(1)}, f32[16,192,192]{2,1,0:T(8,128)}, u32[]{:S(2)}) copy-start(f32[16,192,192]{2,1,0:T(8,128)} %copy-done.1) | copy-start | bytes 7077892
  309.7 23.5 %copy-start.4 = (f32[16,192,192]{2,1,0:T(8,128)S(1)}, f32[16,192,192]{2,1,0:T(8,128)}, u32[]{:S(2)}) copy-start(f32[16,192,192]{2,1,0:T(8,128)} %all-reduce.2.cloned.1.call-done) | copy-start | bytes 7077892
Sparse Core Ops, SparseCore 0:
  48.6 86.9 all-reduce.1
where the time goes:
time: 347 us; the launch traced here: 342 us
  waiting for transfers between devices  162 us (47%)
  matrix products  95.5 us (28%)
  other arithmetic  26.6 us (8%)
  local copies, waits for them, and re-layouts  25 us (7%)
  starting transfers between devices  19.1 us (6%)
  between operations  14.6 us (4%)
    psum x1, waiting for transfers between devices, per_device(): exchange_ints = lax.psum(partial_ints, 'aux')  87.1 us
    ppermute x3, waiting for transfers between devices, with_halo(): lax.ppermute(head, axis, [((i + 1) % count, i) for i in range(ends)])  68.2 us
    dot_general x2, matrix products, transformed_product(): jnp.einsum('pn,pnad->pad', weights, outer_part, precision=lax.Precision.H...  46.8 us
    dot_general x2, matrix products, transformed_product(): jnp.einsum('pnab,pnbc->pnac', side_blocks, gathered, precision=lax.Precis...  19.3 us
    dot_general x2, matrix products, transformed_product(): jnp.einsum('pnac,pndc->pnad', inner_part, side_blocks, precision=lax.Prec...  16.1 us
    concatenate x2, other arithmetic, with_halo(): jnp.concatenate([lax.ppermute(tail, axis, [(i, (i + 1) % count) for i in...  16 us
    gather x2, local copies, waits for them, and re-layouts, coupling(): gathered = jnp.take(padded_amps, local_rows, axis=0)  14.8 us
    ppermute x3, starting transfers between devices, with_halo(): lax.ppermute(tail, axis, [(i, (i + 1) % count) for i in range(ends)])  12.6 us
  transfers between devices with their start and end apart: 7, of which 6 were waited for; matrix products, arithmetic and copies ran while one was open for 2% of the time, Pallas kernels for 0%

commit v1 on v0

--- a/solution.py
+++ b/solution.py
@@ -95,7 +95,8 @@
         "pqa,pqb->pab", left_half, right_half, preferred_element_type=jnp.float32
     )
     mask_float = natural_orbital_mask.astype(jnp.float32)
-    exchange_ints = lax.psum(partial_ints, "aux")
+    pieces = lax.all_gather(partial_ints, "aux", axis=0, tiled=False)
+    exchange_ints = pieces.sum(axis=0)
     denominator = pno_energy[:, :, None] + pno_energy[:, None, :]
     side_blocks = margin.astype(jnp.float32) * mask_float[:, None, :, None]
     local_rows = neighbour_pairs - (position - 1) * pair_dev

time: 347 us -> 390 us (1.12)
  waiting for transfers between devices: 162 us -> 198 us
  other arithmetic: 26.6 us -> 33.1 us
    all_gather x0 -> x1, waiting for transfers between devices: none -> 122 us  [per_device(): pieces = lax.all_gather(partial_ints, 'aux', axis=0, tiled=False)]
    psum x1 -> x0, waiting for transfers between devices: 87.1 us -> none  [per_device(): exchange_ints = lax.psum(partial_ints, 'aux')]
    reduce_sum x0 -> x1, other arithmetic: none -> 6.19 us  [per_device(): exchange_ints = pieces.sum(axis=0)]
where the time goes in v1:
time: 390 us; the launch traced here: 385 us
  waiting for transfers between devices  198 us (51%)
  matrix products  95.6 us (25%)
  other arithmetic  33.1 us (8%)
  local copies, waits for them, and re-layouts  25.3 us (6%)
  starting transfers between devices  18.5 us (5%)
  between operations  14.5 us (4%)
    all_gather x1, waiting for transfers between devices, per_device(): pieces = lax.all_gather(partial_ints, 'aux', axis=0, tiled=False)  122 us
    ppermute x3, waiting for transfers between devices, with_halo(): lax.ppermute(head, axis, [((i + 1) % count, i) for i in range(ends)])  68.8 us
    dot_general x2, matrix products, transformed_product(): jnp.einsum('pn,pnad->pad', weights, outer_part, precision=lax.Precision.H...  46.7 us
    dot_general x2, matrix products, transformed_product(): jnp.einsum('pnab,pnbc->pnac', side_blocks, gathered, precision=lax.Precis...  19.4 us
    concatenate x2, other arithmetic, with_halo(): jnp.concatenate([lax.ppermute(tail, axis, [(i, (i + 1) % count) for i in...  16.2 us
    dot_general x2, matrix products, transformed_product(): jnp.einsum('pnac,pndc->pnad', inner_part, side_blocks, precision=lax.Prec...  16.1 us
    gather x2, local copies, waits for them, and re-layouts, coupling(): gathered = jnp.take(padded_amps, local_rows, axis=0)  14.7 us
    ppermute x3, starting transfers between devices, with_halo(): lax.ppermute(tail, axis, [(i, (i + 1) % count) for i in range(ends)])  12.1 us
  transfers between devices with their start and end apart: 7, of which 6 were waited for; matrix products, arithmetic and copies ran while one was open for 2% of the time, Pallas kernels for 0%

profile of v1, /device:TPU:1, one launch (start us, length us, event | category | flops | bytes accessed | tf_op | source)
XLA Modules:
  0.0 384.6 jit_solution(2428591143477013721)
XLA Ops:
  7.2 4.6 %collective-permute-start = (bf16[4,512,256]{2,1,0:T(8,128)(2,1)}, bf16[4,512,256]{2,1,0:T(8,128)(2,1)}, u32[]{:S(2)}, u32[]{:S(2)}) collective-permute-start(bf16[4,512,256]{2,1,0:T(8,128)(2,1)} %param.12), channel_id=1, source_target_pairs={{0,1},{1,2},{2,3},{3,4},{4,5},{5,6},{6,7},{8,9},{9,10},{10,11},{11... | collective-permute-start | bytes 3145736 | tf_op jit(solution)/shard_map/ppermute | solution.py:18
  11.8 1.9 collective-permute-start.1
  15.2 3.4 copy_select_fusion
  18.6 5.2 %collective-permute-done = bf16[4,512,256]{2,1,0:T(8,128)(2,1)} collective-permute-done((bf16[4,512,256]{2,1,0:T(8,128)(2,1)}, bf16[4,512,256]{2,1,0:T(8,128)(2,1)}, u32[]{:S(2)}, u32[]{:S(2)}) %collective-permute-start) | collective-permute-done | bytes 1048608 | tf_op jit(solution)/shard_map/ppermute | solution.py:18
  25.2 3.0 collective-permute-done.1
  28.3 1.3 constant_dynamic-update-slice_fusion
  29.6 2.8 gather_fusion.1
  32.3 2.8 gather_fusion
  35.1 6.1 %fusion.10 = bf16[16,512,192]{1,2,0:T(8,128)(2,1)} fusion(bf16[16,512,256]{2,1,0:T(8,128)(2,1)} %gather_fusion.1, pred[16]{0:T(512)(128)(4,1)S(1)} %get-tuple-element.10, bf16[16,2,256,192]{2,3,0,1:T(8,128)(2,1)} %copy_select_fusion), kind=kOutput, calls=%fused_computation.22 | convolution fusion | flops 807403520 | bytes 8912912 | tf_op jit(solution)/shard_map/cyg,cgh->cyh/dot_general | solution.py:88
  41.2 7.3 %fusion.29 = f32[16,192,192]{2,1,0:T(8,128)} fusion(bf16[16,512,192]{1,2,0:T(8,128)(2,1)} %fusion.10, bf16[16,512,256]{2,1,0:T(8,128)(2,1)} %gather_fusion, pred[16]{0:T(512)(128)(4,1)S(1)} %get-tuple-element.6, bf16[16,2,256,192]{2,3,0,1:T(8,128)(2,1)S(1)} %copy-done.7), kind=kOutput, calls=%fused_computation.42 | convolution fusion | flops 1412956160 | bytes 11272704 | tf_op jit(solution)/shard_map/pqa,pqb->pab/dot_general | solution.py:94
  48.5 122.4 %all-gather.3.cloned.1.call-done = f32[64,192,192]{2,1,0:T(8,128)} async-done(((f32[16,192,192]{2,1,0:T(8,128)}), f32[64,192,192]{2,1,0:T(8,128)}) %all-gather.3.cloned.1.call-update) | async-done | bytes 9437200 | tf_op jit(solution)/shard_map/all_gather | solution.py:98
  170.9 6.2 %reduce_sum.9 = f32[16,192,192]{2,1,0:T(8,128)S(1)} reduce(f32[4,16,192,192]{3,2,1,0:T(8,128)} %bitcast.28, f32[]{:T(128)} %constant.29.clone.1), dimensions={0}, to_apply=%region_0.2 | reduce | flops 1769472 | bytes 11796484 | tf_op jit(solution)/shard_map/reduce_sum | solution.py:99
  177.1 2.4 fusion.17
  179.8 2.6 collective-permute-start.3
  182.3 3.2 collective-permute-start.2
  185.9 32.8 %collective-permute-done.3 = f32[16,192,192]{2,1,0:T(8,128)} collective-permute-done((f32[16,192,192]{2,1,0:T(8,128)}, f32[16,192,192]{2,1,0:T(8,128)}, u32[]{:S(2)}, u32[]{:S(2)}) %collective-permute-start.3) | collective-permute-done | bytes 2359328 | tf_op jit(solution)/shard_map/ppermute | solution.py:20
  219.9 7.7 %pad_maximum_fusion = f32[48,192,192]{2,1,0:T(8,128)} fusion(f32[16,192,192]{2,1,0:T(8,128)} %collective-permute-done.3, f32[16,192,192]{2,1,0:T(8,128)} %fusion.17, f32[16,192,192]{2,1,0:T(8,128)S(1)} %collective-permute-done.2), kind=kLoop, calls=%fused_computation.4 | loop fusion | flops 3538944 | bytes 14155776 | tf_op jit(solution)/shard_map/concatenate | solution.py:16
  227.6 7.4 %gather_fusion.2 = f32[32,192,192]{2,1,0:T(8,128)} fusion(f32[48,192,192]{2,1,0:T(8,128)} %pad_maximum_fusion, s32[1024]{0:T(1024)S(1)} %pad_clamp_fusion), kind=kCustom, calls=%fused_computation.1.clone | custom fusion | bytes 9437312 | tf_op jit(solution)/shard_map/jit(_take)/gather | solution.py:106
  235.0 9.5 %fusion.2 = f32[16,2,192,192]{3,2,1,0:T(8,128)S(1)} fusion(f32[16,2,192,192]{3,2,1,0:T(8,128)} %bitcast.27, bf16[16,2,192,192]{3,2,1,0:T(8,128)(2,1)S(1)} %copy-done, f32[16,192]{1,0:T(8,128)S(1)} %get-tuple-element.12, pred[16,2]{1,0:T(8,128)(4,1)S(1)} %copy.19), kind=kOutput, calls=%fused_computation.13 | convolution fusion | flops 2721447936 | bytes 11808800 | tf_op jit(solution)/shard_map/pnab,pnbc->pnac/dot_general | solution.py:41
  244.5 8.0 %fusion.5 = f32[16,2,192,192]{3,2,1,0:T(8,128)S(1)} fusion(f32[16,2,192,192]{3,2,1,0:T(8,128)S(1)} %fusion.2, bf16[16,2,192,192]{3,2,1,0:T(8,128)(2,1)S(1)} %copy-done, f32[16,192]{1,0:T(8,128)S(1)} %get-tuple-element.12), kind=kOutput, calls=%fused_computation.17 | convolution fusion | flops 2720268288 | bytes 11808768 | tf_op jit(solution)/shard_map/pnac,pndc->pnad/dot_general | solution.py:44
  252.6 23.4 %fusion.8 = f32[16,1,192,192]{3,1,2,0:T(1,128)S(1)} fusion(f32[16,2,1,1]{1,2,3,0:T(1,128)S(1)} %copy.24, f32[16,2,192,192]{3,2,1,0:T(8,128)S(1)} %fusion.5), kind=kOutput, calls=%fused_computation.20 | convolution fusion | flops 14155776 | bytes 7078016 | tf_op jit(solution)/shard_map/pn,pnad->pad/dot_general | solution.py:47
  276.0 1.4 fusion.20
  277.4 1.9 collective-permute-start.5
  279.3 4.3 %collective-permute-start.4 = (f32[16,192,192]{2,1,0:T(8,128)S(1)}, f32[16,192,192]{2,1,0:T(8,128)}, u32[]{:S(2)}, u32[]{:S(2)}) collective-permute-start(f32[16,192,192]{2,1,0:T(8,128)S(1)} %fusion.20), channel_id=1, source_target_pairs={{0,1},{1,2},{2,3},{3,4},{4,5},{5,6},{6,7},{8,9},{9,10},{10,11},{11... | collective-permute-start | bytes 7077896 | tf_op jit(solution)/shard_map/ppermute | solution.py:18
  283.6 33.0 %collective-permute-done.5 = f32[16,192,192]{2,1,0:T(8,128)S(1)} collective-permute-done((f32[16,192,192]{2,1,0:T(8,128)S(1)}, f32[16,192,192]{2,1,0:T(8,128)S(1)}, u32[]{:S(2)}, u32[]{:S(2)}) %collective-permute-start.5) | collective-permute-done | bytes 2359328 | tf_op jit(solution)/shard_map/ppermute | solution.py:20
  316.6 1.7 copy-done.6
  318.3 8.5 %pad_maximum_fusion.1 = f32[48,192,192]{2,1,0:T(8,128)} fusion(f32[16,192,192]{2,1,0:T(8,128)} %copy-done.6, f32[16,192,192]{2,1,0:T(8,128)} %copy-done.4, f32[16,192,192]{2,1,0:T(8,128)} %collective-permute-done.4), kind=kLoop, calls=%fused_computation.5 | loop fusion | flops 3538944 | bytes 14155776 | tf_op jit(solution)/shard_map/concatenate | solution.py:16
  326.8 7.3 %gather_fusion.3 = f32[32,192,192]{2,1,0:T(8,128)} fusion(f32[48,192,192]{2,1,0:T(8,128)} %pad_maximum_fusion.1, s32[1024]{0:T(1024)S(1)} %pad_clamp_fusion), kind=kCustom, calls=%fused_computation.3.clone | custom fusion | bytes 9437312 | tf_op jit(solution)/shard_map/jit(_take)/gather | solution.py:106
  334.1 9.9 %fusion = f32[16,2,192,192]{3,2,1,0:T(8,128)S(1)} fusion(f32[16,2,192,192]{3,2,1,0:T(8,128)} %bitcast.26, bf16[16,2,192,192]{3,2,1,0:T(8,128)(2,1)S(1)} %copy-done, f32[16,192]{1,0:T(8,128)S(1)} %get-tuple-element.12, pred[16,2]{1,0:T(8,128)(4,1)S(1)} %copy.19), kind=kOutput, calls=%fused_computation.11 | convolution fusion | flops 2721447936 | bytes 11808800 | tf_op jit(solution)/shard_map/pnab,pnbc->pnac/dot_general | solution.py:41
  344.1 8.0 %fusion.4 = f32[16,2,192,192]{3,2,1,0:T(8,128)S(1)} fusion(f32[16,2,192,192]{3,2,1,0:T(8,128)S(1)} %fusion, bf16[16,2,192,192]{3,2,1,0:T(8,128)(2,1)S(1)} %copy-done, f32[16,192]{1,0:T(8,128)S(1)} %get-tuple-element.12), kind=kOutput, calls=%fused_computation.16 | convolution fusion | flops 2720268288 | bytes 11808768 | tf_op jit(solution)/shard_map/pnac,pndc->pnad/dot_general | solution.py:44
  352.1 23.3 %fusion.6 = f32[16,1,192,192]{3,1,2,0:T(1,128)S(1)} fusion(f32[16,2,1,1]{1,2,3,0:T(1,128)S(1)} %copy.24, f32[16,2,192,192]{3,2,1,0:T(8,128)S(1)} %fusion.4), kind=kOutput, calls=%fused_computation.18 | convolution fusion | flops 14155776 | bytes 7078016 | tf_op jit(solution)/shard_map/pn,pnad->pad/dot_general | solution.py:47
  375.5 2.0 fusion.22
  (40 shorter events, 4.7 us)
Async XLA Ops:
  7.2 163.7 %all-gather.3.cloned.1.call-start = ((), (), s32[]{:S(2)}) async-start(), calls=%async_computation | async-start | bytes 15728640 | tf_op jit(solution)/shard_map/all_gather | solution.py:98
  7.2 16.6 %collective-permute-start = (bf16[4,512,256]{2,1,0:T(8,128)(2,1)}, bf16[4,512,256]{2,1,0:T(8,128)(2,1)}, u32[]{:S(2)}, u32[]{:S(2)}) collective-permute-start(bf16[4,512,256]{2,1,0:T(8,128)(2,1)} %param.12), channel_id=1, source_target_pairs={{0,1},{1,2},{2,3},{3,4},{4,5},{5,6},{6,7},{8,9},{9,10},{10,11},{11... | collective-permute-start | bytes 3145736 | tf_op jit(solution)/shard_map/ppermute | solution.py:18
  11.8 16.4 %collective-permute-start.1 = (bf16[4,512,256]{2,1,0:T(8,128)(2,1)}, bf16[4,512,256]{2,1,0:T(8,128)(2,1)}, u32[]{:S(2)}, u32[]{:S(2)}) collective-permute-start(bf16[4,512,256]{2,1,0:T(8,128)(2,1)} %param.12), channel_id=1, source_target_pairs={{1,0},{2,1},{3,2},{4,3},{5,4},{6,5},{7,6},{9,8},{10,9},{11,10},{12... | collective-permute-start | bytes 3145736 | tf_op jit(solution)/shard_map/ppermute | solution.py:20
  15.2 10.0 %copy-start.8 = (bf16[4,512,256]{2,1,0:T(8,128)(2,1)S(1)}, bf16[4,512,256]{2,1,0:T(8,128)(2,1)}, u32[]{:S(2)}) copy-start(bf16[4,512,256]{2,1,0:T(8,128)(2,1)} %param.12) | copy-start | bytes 3145732
  35.1 6.1 %copy-start.7 = (bf16[16,2,256,192]{2,3,0,1:T(8,128)(2,1)S(1)}, bf16[16,2,256,192]{2,3,0,1:T(8,128)(2,1)}, u32[]{:S(2)}) copy-start(bf16[16,2,256,192]{2,3,0,1:T(8,128)(2,1)} %copy_select_fusion) | copy-start | bytes 9437188
  170.9 6.2 %copy-start.9 = (f32[16,192]{1,0:T(8,128)S(1)}, f32[16,192]{1,0:T(8,128)}, u32[]{:S(2)}) copy-start(f32[16,192]{1,0:T(8,128)} %param.16) | copy-start | bytes 36868
  177.1 2.7 copy-start.1
  177.1 8.4 %copy-start.10 = (s32[16,2]{0,1:T(2,128)S(1)}, s32[16,2]{0,1:T(2,128)}, u32[]{:S(2)}) copy-start(s32[16,2]{0,1:T(2,128)} %param.18) | copy-start | bytes 388
  177.1 8.5 %copy-start.11 = (f32[16,2]{0,1:T(2,128)S(1)}, f32[16,2]{0,1:T(2,128)}, u32[]{:S(2)}) copy-start(f32[16,2]{0,1:T(2,128)} %param.19) | copy-start | bytes 388
  179.8 38.9 %collective-permute-start.3 = (f32[16,192,192]{2,1,0:T(8,128)}, f32[16,192,192]{2,1,0:T(8,128)}, u32[]{:S(2)}, u32[]{:S(2)}) collective-permute-start(f32[16,192,192]{2,1,0:T(8,128)} %fusion.17), channel_id=1, source_target_pairs={{1,0},{2,1},{3,2},{4,3},{5,4},{6,5},{7,6},{9,8},{10,9},{11,10},{12... | collective-permute-start | bytes 7077896 | tf_op jit(solution)/shard_map/ppermute | solution.py:20
  182.3 37.5 %collective-permute-start.2 = (f32[16,192,192]{2,1,0:T(8,128)}, f32[16,192,192]{2,1,0:T(8,128)S(1)}, u32[]{:S(2)}, u32[]{:S(2)}) collective-permute-start(f32[16,192,192]{2,1,0:T(8,128)} %fusion.17), channel_id=1, source_target_pairs={{0,1},{1,2},{2,3},{3,4},{4,5},{5,6},{6,7},{8,9},{9,10},{10,11},{11... | collective-permute-start | bytes 7077896 | tf_op jit(solution)/shard_map/ppermute | solution.py:18
  227.5 7.5 %copy-start = (bf16[16,2,192,192]{3,2,1,0:T(8,128)(2,1)S(1)}, bf16[16,2,192,192]{3,2,1,0:T(8,128)(2,1)}, u32[]{:S(2)}) copy-start(bf16[16,2,192,192]{3,2,1,0:T(8,128)(2,1)} %param.17) | copy-start | bytes 7077892
  252.6 23.4 %copy-start.2 = (f32[16,192,192]{2,1,0:T(8,128)S(1)}, f32[16,192,192]{2,1,0:T(8,128)}, u32[]{:S(2)}) copy-start(f32[16,192,192]{2,1,0:T(8,128)} %copy-done.1) | copy-start | bytes 7077892
  277.4 1.9 copy-start.4
  277.4 39.2 %collective-permute-start.5 = (f32[16,192,192]{2,1,0:T(8,128)S(1)}, f32[16,192,192]{2,1,0:T(8,128)S(1)}, u32[]{:S(2)}, u32[]{:S(2)}) collective-permute-start(f32[16,192,192]{2,1,0:T(8,128)S(1)} %fusion.20), channel_id=1, source_target_pairs={{1,0},{2,1},{3,2},{4,3},{5,4},{6,5},{7,6},{9,8},{10,9},{11,10},{12... | collective-permute-start | bytes 7077896 | tf_op jit(solution)/shard_map/ppermute | solution.py:20
  279.3 39.0 %collective-permute-start.4 = (f32[16,192,192]{2,1,0:T(8,128)S(1)}, f32[16,192,192]{2,1,0:T(8,128)}, u32[]{:S(2)}, u32[]{:S(2)}) collective-permute-start(f32[16,192,192]{2,1,0:T(8,128)S(1)} %fusion.20), channel_id=1, source_target_pairs={{0,1},{1,2},{2,3},{3,4},{4,5},{5,6},{6,7},{8,9},{9,10},{10,11},{11... | collective-permute-start | bytes 7077896 | tf_op jit(solution)/shard_map/ppermute | solution.py:18
  316.6 1.7 copy-start.6
  352.1 23.4 %copy-start.3 = (f32[16,192,192]{2,1,0:T(8,128)S(1)}, f32[16,192,192]{2,1,0:T(8,128)}, u32[]{:S(2)}) copy-start(f32[16,192,192]{2,1,0:T(8,128)} %copy-done.1) | copy-start | bytes 7077892
  352.1 23.4 %copy-start.5 = (f32[16,192,192]{2,1,0:T(8,128)S(1)}, f32[16,192,192]{2,1,0:T(8,128)}, u32[]{:S(2)}) copy-start(f32[16,192,192]{2,1,0:T(8,128)} %copy-done.4) | copy-start | bytes 7077892
Sparse Core Ops, SparseCore 0:
  48.6 122.2 all-gather.2
